TPU v7x, 32 devices: a whole 2x2x4 slice. The times are simulated.
32 devices in a mesh: outer: 4 (over z), inner: 2 (over x), tensor: 4 (over y, core).
Axes of the slice: x: 2, y: 2, z: 4, core: 2. Of those that a mesh axis runs over, the one named last changes fastest.
Arguments:
- hidden_in: bfloat16 [16, 577, 1024], P(('outer', 'inner')), may hold values from -6 to 6
- ln1_gain: float32 [1024], replicated, may hold values from 0.5 to 1.5
- ln1_shift: float32 [1024], replicated, may hold values from -1.5 to 1.5
- w_qkv: bfloat16 [1024, 3, 1024], P(None, None, 'tensor'), may hold values from -0.1875 to 0.1875
- qkv_bias: float32 [2, 1024], P(None, 'tensor'), may hold values from -1.5 to 1.5
- w_out: bfloat16 [1024, 1024], P('tensor'), may hold values from -0.75 to 0.75
- out_bias: float32 [1024], replicated, may hold values from -1.5 to 1.5
- ln2_gain: float32 [1024], replicated, may hold values from 0.5 to 1.5
- ln2_shift: float32 [1024], replicated, may hold values from -1.5 to 1.5
- w_fc1: bfloat16 [1024, 4096], P(None, 'tensor'), may hold values from -0.1875 to 0.1875
- fc1_bias: float32 [4096], P('tensor'), may hold values from -1.5 to 1.5
- w_fc2: bfloat16 [4096, 1024], P('tensor'), may hold values from -0.09375 to 0.09375
- fc2_bias: float32 [1024], replicated, may hold values from -1.5 to 1.5
- flags: int32 [16], P(('outer', 'inner')), may hold values 0 or 1
- out_grad: bfloat16 [16, 577, 1024], P(('outer', 'inner')), may hold values from -6 to 6
Outputs:
- block_out: bfloat16 [16, 577, 1024], P(('outer', 'inner'))
- in_grad: bfloat16 [16, 577, 1024], P(('outer', 'inner'))
- g_ln1_gain: float32 [1024], replicated
- g_ln1_shift: float32 [1024], replicated
- g_w_qkv: float32 [1024, 3, 1024], P(None, None, 'tensor')
- g_qkv_bias: float32 [2, 1024], P(None, 'tensor')
- g_w_out: float32 [1024, 1024], P('tensor')
- g_out_bias: float32 [1024], replicated
- g_ln2_gain: float32 [1024], replicated
- g_ln2_shift: float32 [1024], replicated
- g_w_fc1: float32 [1024, 4096], P(None, 'tensor')
- g_fc1_bias: float32 [4096], P('tensor')
- g_w_fc2: float32 [4096, 1024], P('tensor')
- g_fc2_bias: float32 [1024], replicated
Inputs may be any that keep to these rules, and one draw needn't show every extreme that they name: `flags`: 1 marks an image, 0 a padded slot.
All inputs are finite; a program needn't handle non-finite values. No bound on the sum of `flags` on one device may be relied on, other than what follows from the above.
Results may differ from a plain program's by a relative error of at most 0.012.
Values sent between devices are 32-bit elements; how exact they have to be, the bound alone decides.
No kernel may reach another device: no remote copies, remote signals or barrier semaphores. Data moves between devices by JAX's collectives and lax.ppermute only.
A program may use at most 192 MiB of HBM per device.

v0:
```python
import jax
import jax.numpy as jnp
from jax import lax
from jax.sharding import PartitionSpec as P

HD = 64
norm_eps = 1e-05


def layer_norm(values_in, gain_vec, shift_vec):
    row_mean = jnp.mean(values_in, axis=-1, keepdims=True)
    centered = values_in - row_mean
    row_var = jnp.mean(centered * centered, axis=-1, keepdims=True)
    return centered * lax.rsqrt(row_var + norm_eps) * gain_vec + shift_vec


def quick_gelu(values_in):
    return values_in * jax.nn.sigmoid(1.702 * values_in)


def gelu_slope(values_in):
    sig_val = jax.nn.sigmoid(1.702 * values_in)
    return sig_val + 1.702 * values_in * sig_val * (1.0 - sig_val)


def mat_prod(left, right):
    return jnp.dot(left, right, preferred_element_type=jnp.float32)


def left_contract(left, right):
    return lax.dot_general(
        left, right, (((0,), (0,)), ((), ())), preferred_element_type=jnp.float32
    )


def right_contract(left, right):
    return lax.dot_general(
        left, right, (((1,), (1,)), ((), ())), preferred_element_type=jnp.float32
    )


def col_sum(values_in):
    return jnp.sum(values_in.astype(jnp.float32), axis=0)


def attn_scores(q_heads, k_heads, score_scale):
    return (
        jnp.einsum("bqhd,bkhd->bhqk", q_heads, k_heads, preferred_element_type=jnp.float32)
        * score_scale
    )


def per_device(
    hidden_in,
    ln1_gain,
    ln1_shift,
    w_qkv,
    qkv_bias,
    w_out,
    out_bias,
    ln2_gain,
    ln2_shift,
    w_fc1,
    fc1_bias,
    w_fc2,
    fc2_bias,
    flags,
    out_grad,
):
    img_count, seq_len, model_width = hidden_in.shape
    row_count = img_count * seq_len
    head_cols = w_qkv.shape[2]
    head_count = head_cols // HD
    score_scale = HD ** (-0.5)
    head_shape = (img_count, seq_len, head_count, HD)
    qkv_flat = w_qkv.reshape(model_width, 3 * head_cols)
    x_rows = hidden_in.reshape(row_count, model_width).astype(jnp.float32)
    normed1 = layer_norm(x_rows, ln1_gain, ln1_shift).astype(jnp.bfloat16)
    projected = mat_prod(normed1, qkv_flat).reshape(row_count, 3, head_cols)
    q_heads = (projected[:, 0] + qkv_bias[0]).astype(jnp.bfloat16).reshape(head_shape)
    k_heads = projected[:, 1].astype(jnp.bfloat16).reshape(head_shape)
    v_heads = (projected[:, 2] + qkv_bias[1]).astype(jnp.bfloat16).reshape(head_shape)
    scores = attn_scores(q_heads, k_heads, score_scale)
    log_total = jax.nn.logsumexp(scores, axis=-1, keepdims=True)
    attn_probs = jnp.exp(scores - log_total).astype(jnp.bfloat16)
    attended = jnp.einsum(
        "bhqk,bkhd->bqhd", attn_probs, v_heads, preferred_element_type=jnp.float32
    )
    attended = attended.astype(jnp.bfloat16).reshape(row_count, head_cols)
    attn_total = lax.psum(mat_prod(attended, w_out), "tensor")
    resid_mid = x_rows + attn_total + out_bias
    normed2 = layer_norm(resid_mid, ln2_gain, ln2_shift).astype(jnp.bfloat16)
    pre_act = mat_prod(normed2, w_fc1) + fc1_bias
    gelu_out = quick_gelu(pre_act).astype(jnp.bfloat16)
    mlp_total = lax.psum(mat_prod(gelu_out, w_fc2), "tensor")
    block_out = (resid_mid + mlp_total + fc2_bias).astype(jnp.bfloat16).reshape(hidden_in.shape)
    out_cot = (out_grad.astype(jnp.float32) * flags.astype(jnp.float32)[:, None, None]).reshape(
        row_count, model_width
    )
    g_fc2_bias = jnp.sum(out_cot, axis=0)
    mlp_cot = out_cot.astype(jnp.bfloat16)
    g_w_fc2 = left_contract(gelu_out, mlp_cot)
    pre_grad = (right_contract(mlp_cot, w_fc2) * gelu_slope(pre_act)).astype(jnp.bfloat16)
    g_w_fc1 = left_contract(normed2, pre_grad)
    g_fc1_bias = col_sum(pre_grad)
    norm2_grad = lax.psum(right_contract(pre_grad, w_fc1), "tensor")
    unused_two, norm2_pull = jax.vjp(layer_norm, resid_mid, ln2_gain, ln2_shift)
    mid_from_norm, g_ln2_gain, g_ln2_shift = norm2_pull(norm2_grad)
    resid_grad = out_cot + mid_from_norm
    g_out_bias = jnp.sum(resid_grad, axis=0)
    attn_cot = resid_grad.astype(jnp.bfloat16)
    g_w_out = left_contract(attended, attn_cot)
    attended_grad = right_contract(attn_cot, w_out).astype(jnp.bfloat16).reshape(head_shape)
    again = attn_scores(q_heads, k_heads, score_scale)
    probs_again = jnp.exp(again - log_total)
    probs_low = probs_again.astype(jnp.bfloat16)
    probs_grad = jnp.einsum(
        "bqhd,bkhd->bhqk", attended_grad, v_heads, preferred_element_type=jnp.float32
    )
    row_dot = jnp.sum(probs_again * probs_grad, axis=-1, keepdims=True)
    score_grad = (probs_again * (probs_grad - row_dot)).astype(jnp.bfloat16)
    q_grad = (
        jnp.einsum("bhqk,bkhd->bqhd", score_grad, k_heads, preferred_element_type=jnp.float32)
        * score_scale
    ).astype(jnp.bfloat16)
    k_grad = (
        jnp.einsum("bhqk,bqhd->bkhd", score_grad, q_heads, preferred_element_type=jnp.float32)
        * score_scale
    ).astype(jnp.bfloat16)
    v_grad = jnp.einsum(
        "bhqk,bqhd->bkhd", probs_low, attended_grad, preferred_element_type=jnp.float32
    ).astype(jnp.bfloat16)
    q_rows = q_grad.reshape(row_count, head_cols)
    v_rows = v_grad.reshape(row_count, head_cols)
    qkv_grad = jnp.stack([q_rows, k_grad.reshape(row_count, head_cols), v_rows], axis=1).reshape(
        row_count, 3 * head_cols
    )
    g_w_qkv = left_contract(normed1, qkv_grad).reshape(model_width, 3, head_cols)
    g_qkv_bias = jnp.stack([col_sum(q_rows), col_sum(v_rows)], axis=0)
    norm1_grad = lax.psum(right_contract(qkv_grad, qkv_flat), "tensor")
    unused_one, norm1_pull = jax.vjp(layer_norm, x_rows, ln1_gain, ln1_shift)
    x_from_norm, g_ln1_gain, g_ln1_shift = norm1_pull(norm1_grad)
    in_grad = (resid_grad + x_from_norm).astype(jnp.bfloat16).reshape(hidden_in.shape)
    shares = (
        lax.psum_scatter(g_ln1_gain, "inner", scatter_dimension=0, tiled=True),
        lax.psum_scatter(g_ln1_shift, "inner", scatter_dimension=0, tiled=True),
        lax.psum_scatter(g_w_qkv, "inner", scatter_dimension=0, tiled=True),
        lax.psum_scatter(g_qkv_bias, "inner", scatter_dimension=1, tiled=True),
        lax.psum_scatter(g_w_out, "inner", scatter_dimension=1, tiled=True),
        lax.psum_scatter(g_out_bias, "inner", scatter_dimension=0, tiled=True),
        lax.psum_scatter(g_ln2_gain, "inner", scatter_dimension=0, tiled=True),
        lax.psum_scatter(g_ln2_shift, "inner", scatter_dimension=0, tiled=True),
        lax.psum_scatter(g_w_fc1, "inner", scatter_dimension=0, tiled=True),
        lax.psum_scatter(g_fc1_bias, "inner", scatter_dimension=0, tiled=True),
        lax.psum_scatter(g_w_fc2, "inner", scatter_dimension=1, tiled=True),
        lax.psum_scatter(g_fc2_bias, "inner", scatter_dimension=0, tiled=True),
    )
    shares = lax.psum(
        (
            shares[0],
            shares[1],
            shares[2],
            shares[3],
            shares[4],
            shares[5],
            shares[6],
            shares[7],
            shares[8],
            shares[9],
            shares[10],
            shares[11],
        ),
        "outer",
    )
    (
        s_ln1_gain,
        s_ln1_shift,
        s_w_qkv,
        s_qkv_bias,
        s_w_out,
        s_out_bias,
        s_ln2_gain,
        s_ln2_shift,
        s_w_fc1,
        s_fc1_bias,
        s_w_fc2,
        s_fc2_bias,
    ) = shares
    summed = (
        lax.all_gather(s_ln1_gain, "inner", axis=0, tiled=True),
        lax.all_gather(s_ln1_shift, "inner", axis=0, tiled=True),
        lax.all_gather(s_w_qkv, "inner", axis=0, tiled=True),
        lax.all_gather(s_qkv_bias, "inner", axis=1, tiled=True),
        lax.all_gather(s_w_out, "inner", axis=1, tiled=True),
        lax.all_gather(s_out_bias, "inner", axis=0, tiled=True),
        lax.all_gather(s_ln2_gain, "inner", axis=0, tiled=True),
        lax.all_gather(s_ln2_shift, "inner", axis=0, tiled=True),
        lax.all_gather(s_w_fc1, "inner", axis=0, tiled=True),
        lax.all_gather(s_fc1_bias, "inner", axis=0, tiled=True),
        lax.all_gather(s_w_fc2, "inner", axis=1, tiled=True),
        lax.all_gather(s_fc2_bias, "inner", axis=0, tiled=True),
    )
    return (
        block_out,
        in_grad,
        summed[0],
        summed[1],
        summed[2],
        summed[3],
        summed[4],
        summed[5],
        summed[6],
        summed[7],
        summed[8],
        summed[9],
        summed[10],
        summed[11],
    )


def solution(mesh):
    placed = (
        P(("outer", "inner"), None, None),
        P(),
        P(),
        P(None, None, "tensor"),
        P(None, "tensor"),
        P("tensor", None),
        P(),
        P(),
        P(),
        P(None, "tensor"),
        P("tensor"),
        P("tensor", None),
        P(),
        P(("outer", "inner")),
        P(("outer", "inner"), None, None),
    )
    return jax.shard_map(
        per_device,
        mesh=mesh,
        in_specs=placed,
        out_specs=(
            P(("outer", "inner"), None, None),
            P(("outer", "inner"), None, None),
            P(),
            P(),
            P(None, None, "tensor"),
            P(None, "tensor"),
            P("tensor", None),
            P(),
            P(),
            P(),
            P(None, "tensor"),
            P("tensor"),
            P("tensor", None),
            P(),
        ),
        check_vma=False,
    )
```

profile of v0, /device:TPU:0, one launch (start us, length us, event | category | flops | bytes accessed | tf_op | source)
XLA Modules:
  0.0 1097.4 jit_solution(336543928301203086)
XLA Ops:
  7.3 3.7 convert_reduce_fusion.1
  11.1 3.2 multiply_reduce_fusion.7
  15.2 2.9 copy.115
  18.1 5.7 add_convert_fusion.3
  26.0 3.6 reshape.245
  29.5 4.2 fusion.4
  36.0 2.9 reshape.262
  45.8 3.1 reshape.249
  48.9 3.5 copy.119
  52.4 3.6 multiply_reduce_fusion.1
  64.3 2.7 reshape.224
  67.0 4.2 fusion.34
  71.5 4.8 copy.109
  76.3 3.8 fusion.28
  80.1 3.6 copy.124
  83.7 4.9 reshape.226
  88.7 5.1 reshape.230
  93.8 74.9 %all-reduce.16.cloned.1.call-done = f32[1154,1024]{1,0:T(8,128)} async-done(((f32[1154,1024]{1,0:T(8,128)}), f32[1154,1024]{1,0:T(8,128)}) %all-reduce.16.cloned.1.call-update) | async-done | bytes 4726800 | tf_op jit(solution)/shard_map/psum | solution.py:90
  168.6 4.4 fusion.32
  176.3 3.1 convolution_add_fusion
  179.4 4.6 convert_reduce_fusion
  185.4 4.3 fusion.35
  189.8 94.8 %all-reduce.18.cloned.1.call-done = f32[1154,1024]{1,0:T(8,128)} async-done(((f32[1154,1024]{1,0:T(8,128)}), f32[1154,1024]{1,0:T(8,128)}) %all-reduce.18.cloned.1.call-update) | async-done | bytes 4726800 | tf_op jit(solution)/shard_map/psum | solution.py:106
  284.6 5.4 multiply_reduce_fusion.2
  290.1 3.9 fusion.31
  298.8 8.5 fusion.26
  307.4 8.8 fusion.15
  316.2 4.2 convolution_convert_fusion
  320.4 3.3 reshape.263
  326.1 8.4 convert_reduce_fusion.2
  336.9 3.0 reshape.252
  339.9 8.1 multiply_reduce_fusion
  348.0 6.5 multiply_convert_fusion
  354.5 2.6 copy-done.4
  360.5 3.0 reshape.251
  363.6 4.8 convert_reduce_fusion.3
  376.3 5.7 fusion.2
  382.1 51.6 %reduce-scatter.14.cloned.1.call-done = f32[1024,512]{1,0:T(8,128)} async-done(((f32[1024,1024]{1,0:T(8,128)}), f32[1024,512]{1,0:T(8,128)}) %reduce-scatter.14.cloned.1.call-update) | async-done | bytes 2097168 | tf_op jit(solution)/shard_map/reduce_scatter | solution.py:155
  433.7 46.1 %reduce-scatter.8.cloned.1.call-done = f32[512,3,256]{2,0,1:T(8,128)} async-done(((f32[1024,3,256]{2,0,1:T(8,128)}), f32[512,3,256]{2,0,1:T(8,128)}) %reduce-scatter.8.cloned.1.call-update) | async-done | bytes 1572880 | tf_op jit(solution)/shard_map/reduce_scatter | solution.py:147
  479.9 6.7 fusion.27
  487.7 6.8 convolution_bitcast_fusion
  494.6 210.7 %all-reduce.22.cloned.1.call-done = (f32[512,3,256]{2,0,1:T(8,128)}, f32[256,512]{1,0:T(8,128)}, f32[512,1024]{1,0:T(8,128)}, f32[1024,512]{1,0:T(8,128)}) async-done(((f32[512,3,256]{2,0,1:T(8,128)}, f32[256,512]{1,0:T(8,128)}, f32[512,1024]{1,0:T(8,128)}, f32[1024,512]{1,0:T(8,128)}), (f32[512,3,256]{2,0,1:T(8,128)}, f32[256,512]{1,0:T(8,128)}, f32[512,1024]{1,0:T(8,128)}, ...) | async-done | bytes 6291472 | tf_op jit(solution)/shard_map/psum | solution.py:158
  709.0 8.4 reduce-scatter.16.cloned.1.call-done
  718.3 172.7 %all-reduce.20.cloned.1.call-done = (f32[1154,1024]{1,0:T(8,128)}, f32[1154,1024]{1,0:T(8,128)}) async-done(((f32[1154,1024]{1,0:T(8,128)}, f32[1154,1024]{1,0:T(8,128)}), (f32[1154,1024]{1,0:T(8,128)}, f32[1154,1024]{1,0:T(8,128)})) %all-reduce.20.cloned.1.call-update) | async-done | bytes 9453584 | tf_op jit(solution)/shard_map/psum | solution.py:95
  891.0 6.5 add_convert_fusion.1
  897.5 3.7 reshape.225
  901.2 5.7 copy.140
  906.9 4.3 multiply_reduce_fusion.3
  911.1 8.3 all-reduce.10
  920.0 18.8 %all-reduce.8 = (f32[512]{0:T(512)S(1)}, f32[512]{0:T(512)S(1)}, f32[2,128]{1,0:T(2,128)S(1)}, f32[512]{0:T(512)S(1)}, f32[512]{0:T(512)S(1)}, /*index=5*/f32[512]{0:T(512)S(1)}, f32[512]{0:T(512)S(1)}, f32[512]{0:T(512)S(1)}) all-reduce(f32[512]{0:T(512)S(1)} %dynamic-slice.1, ...), channel_id=1, replica_groups=mesh['outer'=4,'inner'=2,'tensor'=4] {'outer'}, use_global_device_ids=true, to_apply=%region_17.0 | all-reduce | flops 3840 | bytes 30720 | tf_op jit(solution)/shard_map/psum | solution.py:158
  938.8 4.5 all-gather.1
  943.3 4.5 all-gather
  947.9 4.4 all_gather.39
  952.2 4.5 all-gather.2
  956.8 4.4 all-gather.3
  961.1 4.4 all-gather.4
  965.5 4.4 all-gather.5
  969.8 4.6 all-gather.6
  974.5 5.0 fusion.30
  981.5 3.5 reshape.228
  985.0 5.5 copy.141
  990.5 28.3 %all-gather.16.cloned.1.call-done = f32[1024,1024]{1,0:T(8,128)} async-done(((f32[512,1024]{1,0:T(8,128)}), f32[1024,1024]{1,0:T(8,128)}) %all-gather.16.cloned.1.call-update) | async-done | bytes 4194320 | tf_op jit(solution)/shard_map/all_gather | solution.py:198
  1018.8 58.3 %all-gather.18.cloned.1.call-done = f32[1024,1024]{1,0:T(8,128)} async-done(((f32[1024,512]{1,0:T(8,128)}), f32[1024,1024]{1,0:T(8,128)}) %all-gather.18.cloned.1.call-update) | async-done | bytes 4194320 | tf_op jit(solution)/shard_map/all_gather | solution.py:200
  1078.2 3.8 copy.190
  (176 shorter events, 63.6 us)
Async XLA Ops:
  7.2 172.2 %copy-start = (bf16[1024,1024]{1,0:T(8,128)(2,1)S(1)}, bf16[1024,1024]{1,0:T(8,128)(2,1)}, u32[]{:S(2)}) copy-start(bf16[1024,1024]{1,0:T(8,128)(2,1)} %param.26) | copy-start | bytes 6291460
  7.2 10.9 copy-start.18
  7.2 10.9 copy-start.24
  7.2 161.4 %all-reduce.16.cloned.1.call-start = ((), (), s32[]{:S(2)}) async-start(), calls=%async_computation.5 | async-start | bytes 9502720 | tf_op jit(solution)/shard_map/psum | solution.py:90
  7.3 3.8 copy-start.5
  11.0 12.8 %copy-start.11 = (f32[2,577]{0,1:T(8,128)}, f32[2,577]{0,1:T(8,128)S(1)}, u32[]{:S(2)}) copy-start(f32[2,577]{0,1:T(8,128)S(1)} %broadcast_multiply_fusion) | copy-start | bytes 13852
  33.7 2.1 copy-start.25
  56.0 4.4 copy-start.1
  71.2 5.0 copy-start.29
  71.2 213.4 %all-reduce.18.cloned.1.call-start = ((), (), s32[]{:S(2)}) async-start(), calls=%async_computation.6 | async-start | bytes 9502720 | tf_op jit(solution)/shard_map/psum | solution.py:106
  71.5 4.8 copy-start.15
  88.7 80.0 %copy-start.22 = (f32[1024]{0:T(1024)S(1)}, f32[1024]{0:T(1024)}, u32[]{:S(2)}) copy-start(f32[1024]{0:T(1024)} %param.21) | copy-start | bytes 12292
  173.0 6.3 copy-start.2
  173.0 0.7 copy-start.21
  173.1 3.2 copy-start.26
  173.1 3.2 copy-start.27
  173.1 3.2 copy-start.28
  173.1 6.3 slice-start.2
  176.2 3.1 slice-start.3
  179.4 4.6 copy-start.31
  184.0 1.4 copy-start.32
  189.8 192.3 %reduce-scatter.10.cloned.1.call-start = ((), (), s32[]{:S(2)}) async-start(), calls=%async_computation.9 | async-start | bytes 1572864 | tf_op jit(solution)/shard_map/reduce_scatter | solution.py:149
  284.6 5.5 copy-start.7
  284.6 9.4 slice-start.4
  290.1 3.9 slice-start.5
  294.1 2.8 copy-start.9
  294.7 2.2 copy-start.3
  298.7 83.4 %reduce-scatter.12.cloned.1.call-start = ((), (), s32[]{:S(2)}) async-start(), calls=%async_computation.11 | async-start | bytes 6291456 | tf_op jit(solution)/shard_map/reduce_scatter | solution.py:153
  307.3 126.4 %reduce-scatter.14.cloned.1.call-start = ((), (), s32[]{:S(2)}) async-start(), calls=%async_computation.13 | async-start | bytes 6291456 | tf_op jit(solution)/shard_map/reduce_scatter | solution.py:155
  316.2 163.6 %reduce-scatter.8.cloned.1.call-start = ((), (), s32[]{:S(2)}) async-start(), calls=%async_computation.7 | async-start | bytes 4718592 | tf_op jit(solution)/shard_map/reduce_scatter | solution.py:147
  348.0 9.1 copy-start.8
  354.5 2.6 copy-start.4
  357.1 6.5 copy-start.10
  375.1 1.2 copy-start.17
  382.0 323.3 %all-reduce.22.cloned.1.call-start = ((), (), s32[]{:S(2)}) async-start(), calls=%async_computation.17 | async-start | bytes 12582912 | tf_op jit(solution)/shard_map/psum | solution.py:158
  479.9 237.6 %reduce-scatter.16.cloned.1.call-start = ((), (), s32[]{:S(2)}) async-start(), calls=%async_computation.15 | async-start | bytes 196608
  487.6 403.3 %all-reduce.20.cloned.1.call-start = ((), (), s32[]{:S(2)}) async-start(), calls=%async_computation.16 | async-start | bytes 19005440 | tf_op jit(solution)/shard_map/psum | solution.py:95
  494.5 212.9 %copy-start.12 = (f32[2,577]{0,1:T(8,128)S(1)}, f32[2,577]{0,1:T(8,128)}, u32[]{:S(2)}) copy-start(f32[2,577]{0,1:T(8,128)} %copy-done.11) | copy-start | bytes 13852
  494.5 213.1 %copy-start.20 = (f32[2,577]{1,0:T(2,128)S(1)}, f32[2,577]{1,0:T(2,128)}, u32[]{:S(2)}) copy-start(f32[2,577]{1,0:T(2,128)} %get-tuple-element.111) | copy-start | bytes 13852
  494.6 213.2 %copy-start.30 = (u32[32]{0:T(128)S(1)}, u32[32]{0:T(128)}, u32[]{:S(2)}) copy-start(u32[32]{0:T(128)} %constant.32) | copy-start | bytes 388
  494.6 396.4 %copy-start.23 = (f32[1024]{0:T(1024)S(1)}, f32[1024]{0:T(1024)}, u32[]{:S(2)}) copy-start(f32[1024]{0:T(1024)} %param.27) | copy-start | bytes 12292
  494.6 495.9 %all-gather.14.cloned.1.call-start = ((), (), s32[]{:S(2)}) async-start(), calls=%async_computation.10 | async-start | bytes 1572864 | tf_op jit(solution)/shard_map/all_gather | solution.py:194
  705.4 285.1 %all-gather.12.cloned.1.call-start = ((), (), s32[]{:S(2)}) async-start(), calls=%async_computation.8 | async-start | bytes 4718592 | tf_op jit(solution)/shard_map/all_gather | solution.py:192
  706.1 312.7 %all-gather.16.cloned.1.call-start = ((), (), s32[]{:S(2)}) async-start(), calls=%async_computation.12 | async-start | bytes 6291456 | tf_op jit(solution)/shard_map/all_gather | solution.py:198
  706.7 370.4 %all-gather.18.cloned.1.call-start = ((), (), s32[]{:S(2)}) async-start(), calls=%async_computation.14 | async-start | bytes 6291456 | tf_op jit(solution)/shard_map/all_gather | solution.py:200
  897.5 9.4 copy-start.19
  901.2 5.7 copy-start.6
  906.8 72.7 %slice-start = ((s8[4751360]{0:T(1024)(128)(4,1)}), s8[557056]{0:T(1024)(128)(4,1)S(1)}, s32[]{:S(2)}) async-start(s8[4751360]{0:T(1024)(128)(4,1)} %bitcast.68), calls=%async_computation.18 | async-start | bytes 1114112
  974.5 5.1 slice-start.1
  990.5 92.1 %copy-start.16 = (f32[256,1024]{1,0:T(8,128)S(1)}, f32[256,1024]{1,0:T(8,128)}, u32[]{:S(2)}) copy-start(f32[256,1024]{1,0:T(8,128)} %all-gather.14.cloned.1.call-done) | copy-start | bytes 3145732
  1077.1 8.4 copy-start.13
  1082.7 5.4 copy-start.14
Sparse Core Ops, SparseCore 0:
  71.3 97.2 all-reduce.15
  189.9 94.6 all-reduce.17
  298.8 20.5 reduce-scatter.9
  322.1 54.3 reduce-scatter.11
  379.3 54.3 reduce-scatter.13
  436.4 43.4 reduce-scatter.7
  482.4 222.8 all-reduce.21
  708.1 9.2 reduce-scatter.15
  720.0 170.9 all-reduce.19
  892.4 21.4 all-gather.13
  915.4 45.1 all-gather.11
  962.0 56.7 all-gather.15
  1020.3 56.6 all-gather.17
where the time goes:
time: 1100 us
  waiting for transfers between devices  748 us (68%)
  local copies, waits for them, and re-layouts  120 us (11%)
  matrix products  92 us (8%)
  blocking collectives  62.8 us (6%)
  other arithmetic  58.5 us (5%)
  between operations  15.5 us (1%)
    psum x1, waiting for transfers between devices, per_device(): lax.psum((shares[0], shares[1], shares[2], shares[3], shares[4], shares[5...  211 us
    psum x1, waiting for transfers between devices, per_device(): mlp_total = lax.psum(mat_prod(gelu_out, w_fc2), 'tensor')  173 us
    psum x1, waiting for transfers between devices, per_device(): norm2_grad = lax.psum(right_contract(pre_grad, w_fc1), 'tensor')  94.8 us
    psum x1, waiting for transfers between devices, per_device(): attn_total = lax.psum(mat_prod(attended, w_out), 'tensor')  74.9 us
    all_gather x1, waiting for transfers between devices, per_device(): lax.all_gather(s_w_fc2, 'inner', axis=1, tiled=True)  58.3 us
    reduce_scatter x1, waiting for transfers between devices, per_device(): lax.psum_scatter(g_w_fc2, 'inner', scatter_dimension=1, tiled=True)  51.6 us
    reduce_scatter x1, waiting for transfers between devices, per_device(): lax.psum_scatter(g_w_qkv, 'inner', scatter_dimension=0, tiled=True)  46.1 us
    unnamed x106, local copies, waits for them, and re-layouts  45.1 us
  transfers between devices with their start and end apart: 13, of which 9 were waited for; matrix products, arithmetic and copies ran while one was open for 14% of the time, Pallas kernels for 0%

commit v1 on v0

--- a/solution.py
+++ b/solution.py
@@ -2,6 +2,7 @@
 import jax.numpy as jnp
 from jax import lax
 from jax.sharding import PartitionSpec as P
+from jax.lax import all_gather
 
 HD = 64
 norm_eps = 1e-05
@@ -87,7 +88,8 @@
         "bhqk,bkhd->bqhd", attn_probs, v_heads, preferred_element_type=jnp.float32
     )
     attended = attended.astype(jnp.bfloat16).reshape(row_count, head_cols)
-    attn_total = lax.psum(mat_prod(attended, w_out), "tensor")
+    local = mat_prod(attended, w_out)
+    attn_total = jnp.sum(all_gather(local, "tensor"), 0)
     resid_mid = x_rows + attn_total + out_bias
     normed2 = layer_norm(resid_mid, ln2_gain, ln2_shift).astype(jnp.bfloat16)
     pre_act = mat_prod(normed2, w_fc1) + fc1_bias

time: 1100 us -> 1150 us (1.045)
  waiting for transfers between devices: 748 us -> 772 us
  other arithmetic: 58.5 us -> 80.7 us
    all_gather x0 -> x1, waiting for transfers between devices: none -> 96.9 us  [per_device(): attn_total = jnp.sum(all_gather(local, 'tensor'), 0)]
    psum x1 -> x0, waiting for transfers between devices: 74.9 us -> none  [per_device(): attn_total = lax.psum(mat_prod(attended, w_out), 'tensor')]
    unnamed x106 -> x109, local copies, waits for them, and re-layouts: 45.1 us -> 43 us
where the time goes in v1:
time: 1150 us; the launch traced here: 1140 us
  waiting for transfers between devices  772 us (67%)
  local copies, waits for them, and re-layouts  115 us (10%)
  matrix products  94 us (8%)
  other arithmetic  80.7 us (7%)
  blocking collectives  62.6 us (5%)
  between operations  15.4 us (1%)
    psum x1, waiting for transfers between devices, per_device(): lax.psum((shares[0], shares[1], shares[2], shares[3], shares[4], shares[5...  211 us
    psum x1, waiting for transfers between devices, per_device(): mlp_total = lax.psum(mat_prod(gelu_out, w_fc2), 'tensor')  173 us
    all_gather x1, waiting for transfers between devices, per_device(): attn_total = jnp.sum(all_gather(local, 'tensor'), 0)  96.9 us
    psum x1, waiting for transfers between devices, per_device(): norm2_grad = lax.psum(right_contract(pre_grad, w_fc1), 'tensor')  94.7 us
    all_gather x1, waiting for transfers between devices, per_device(): lax.all_gather(s_w_fc2, 'inner', axis=1, tiled=True)  58.3 us
    reduce_scatter x1, waiting for transfers between devices, per_device(): lax.psum_scatter(g_w_fc2, 'inner', scatter_dimension=1, tiled=True)  53.8 us
    reduce_scatter x1, waiting for transfers between devices, per_device(): lax.psum_scatter(g_w_qkv, 'inner', scatter_dimension=0, tiled=True)  46.1 us
    unnamed x109, local copies, waits for them, and re-layouts  43 us
  transfers between devices with their start and end apart: 13, of which 9 were waited for; matrix products, arithmetic and copies ran while one was open for 14% of the time, Pallas kernels for 0%

profile of v1, /device:TPU:0, one launch (start us, length us, event | category | flops | bytes accessed | tf_op | source)
XLA Modules:
  0.0 1141.4 jit_solution(10656330114735585893)
XLA Ops:
  9.8 2.6 multiply_reduce_fusion.3
  12.9 2.6 copy.105
  15.5 3.6 add_convert_fusion
  19.1 3.6 reshape.278
  22.6 4.2 fusion.5
  29.1 2.9 reshape.295
  38.9 3.6 reshape.282
  42.5 3.0 copy.109
  45.6 3.6 multiply_reduce_fusion.1
  59.5 4.0 convolution_bitcast_fusion.1
  64.0 5.8 fusion.28
  69.8 4.0 copy.114
  73.8 6.1 reshape.255
  79.9 4.9 copy_convert_fusion
  84.8 5.4 reshape.259
  90.2 96.9 %all-gather.23.cloned.1.call-done = f32[4,1154,1024]{2,1,0:T(8,128)} async-done(((f32[1,1154,1024]{2,1,0:T(8,128)}), f32[4,1154,1024]{2,1,0:T(8,128)}) %all-gather.23.cloned.1.call-update) | async-done | bytes 18907152 | tf_op jit(solution)/shard_map/all_gather | solution.py:92
  187.1 11.5 %reduce_sum.183 = f32[1154,1024]{1,0:T(8,128)} reduce(f32[4,1154,1024]{2,1,0:T(8,128)} %all-gather.23.cloned.1.call-done, f32[]{:T(128)} %constant.8.clone.1), dimensions={0}, to_apply=%region_4.0 | reduce | flops 3545088 | bytes 23633924 | tf_op jit(solution)/shard_map/reduce_sum | solution.py:92
  198.6 5.0 reduce_sum.184
  203.6 4.2 fusion.2
  210.1 7.6 add_add_fusion.4
  217.9 5.9 convolution_add_fusion
  223.8 4.4 convert_reduce_fusion
  229.6 4.4 fusion.33
  234.1 94.7 %all-reduce.15.cloned.1.call-done = f32[1154,1024]{1,0:T(8,128)} async-done(((f32[1154,1024]{1,0:T(8,128)}), f32[1154,1024]{1,0:T(8,128)}) %all-reduce.15.cloned.1.call-update) | async-done | bytes 4726800 | tf_op jit(solution)/shard_map/psum | solution.py:108
  328.7 5.4 multiply_reduce_fusion.4
  334.2 3.9 fusion.31
  342.8 8.5 fusion.26
  351.4 8.8 fusion.16
  360.3 4.0 convolution_convert_fusion
  368.4 8.4 convert_reduce_fusion.2
  379.2 2.9 reshape.285
  382.1 7.8 multiply_reduce_fusion
  389.9 6.4 multiply_convert_fusion
  396.4 2.6 copy-done.4
  402.3 3.0 reshape.284
  405.4 4.7 convert_reduce_fusion.3
  418.1 5.7 fusion.3
  423.8 53.8 %reduce-scatter.14.cloned.1.call-done = f32[1024,512]{1,0:T(8,128)} async-done(((f32[1024,1024]{1,0:T(8,128)}), f32[1024,512]{1,0:T(8,128)}) %reduce-scatter.14.cloned.1.call-update) | async-done | bytes 2097168 | tf_op jit(solution)/shard_map/reduce_scatter | solution.py:157
  477.7 46.1 %reduce-scatter.8.cloned.1.call-done = f32[512,3,256]{2,0,1:T(8,128)} async-done(((f32[1024,3,256]{2,0,1:T(8,128)}), f32[512,3,256]{2,0,1:T(8,128)}) %reduce-scatter.8.cloned.1.call-update) | async-done | bytes 1572880 | tf_op jit(solution)/shard_map/reduce_scatter | solution.py:149
  523.9 6.8 fusion.27
  531.7 6.8 convolution_bitcast_fusion
  538.6 210.7 %all-reduce.19.cloned.1.call-done = (f32[512,3,256]{2,0,1:T(8,128)}, f32[256,512]{1,0:T(8,128)}, f32[512,1024]{1,0:T(8,128)}, f32[1024,512]{1,0:T(8,128)}) async-done(((f32[512,3,256]{2,0,1:T(8,128)}, f32[256,512]{1,0:T(8,128)}, f32[512,1024]{1,0:T(8,128)}, f32[1024,512]{1,0:T(8,128)}), (f32[512,3,256]{2,0,1:T(8,128)}, f32[256,512]{1,0:T(8,128)}, f32[512,1024]{1,0:T(8,128)}, ...) | async-done | bytes 6291472 | tf_op jit(solution)/shard_map/psum | solution.py:160
  752.9 8.6 reduce-scatter.16.cloned.1.call-done
  762.3 172.7 %all-reduce.17.cloned.1.call-done = (f32[1154,1024]{1,0:T(8,128)}, f32[1154,1024]{1,0:T(8,128)}) async-done(((f32[1154,1024]{1,0:T(8,128)}, f32[1154,1024]{1,0:T(8,128)}), (f32[1154,1024]{1,0:T(8,128)}, f32[1154,1024]{1,0:T(8,128)})) %all-reduce.17.cloned.1.call-update) | async-done | bytes 9453584 | tf_op jit(solution)/shard_map/psum | solution.py:97
  935.0 6.5 add_convert_fusion.2
  941.5 3.7 reshape.254
  945.2 5.7 copy.130
  950.9 4.3 multiply_reduce_fusion.5
  955.2 8.3 all-reduce.10
  964.0 18.8 %all-reduce.8 = (f32[512]{0:T(512)S(1)}, f32[512]{0:T(512)S(1)}, f32[2,128]{1,0:T(2,128)S(1)}, f32[512]{0:T(512)S(1)}, f32[512]{0:T(512)S(1)}, /*index=5*/f32[512]{0:T(512)S(1)}, f32[512]{0:T(512)S(1)}, f32[512]{0:T(512)S(1)}) all-reduce(f32[512]{0:T(512)S(1)} %dynamic-slice.1, ...), channel_id=1, replica_groups=mesh['outer'=4,'inner'=2,'tensor'=4] {'outer'}, use_global_device_ids=true, to_apply=%region_17.0 | all-reduce | flops 3840 | bytes 30720 | tf_op jit(solution)/shard_map/psum | solution.py:160
  982.8 4.5 all-gather.3
  987.4 4.5 all-gather.2
  991.9 4.4 all_gather.47
  996.3 4.5 all-gather.4
  1000.8 4.4 all-gather.5
  1005.2 4.4 all-gather.6
  1009.5 4.4 all-gather.7
  1013.9 4.4 all-gather.8
  1018.3 5.1 fusion.30
  1025.3 3.5 reshape.257
  1028.8 5.5 copy.131
  1034.4 28.4 %all-gather.19.cloned.1.call-done = f32[1024,1024]{1,0:T(8,128)} async-done(((f32[512,1024]{1,0:T(8,128)}), f32[1024,1024]{1,0:T(8,128)}) %all-gather.19.cloned.1.call-update) | async-done | bytes 4194320 | tf_op jit(solution)/shard_map/all_gather | solution.py:200
  1062.8 58.3 %all-gather.21.cloned.1.call-done = f32[1024,1024]{1,0:T(8,128)} async-done(((f32[1024,512]{1,0:T(8,128)}), f32[1024,1024]{1,0:T(8,128)}) %all-gather.21.cloned.1.call-update) | async-done | bytes 4194320 | tf_op jit(solution)/shard_map/all_gather | solution.py:202
  1122.3 3.8 copy.184
  (182 shorter events, 66.6 us)
Async XLA Ops:
  7.2 216.6 %copy-start = (bf16[1024,1024]{1,0:T(8,128)(2,1)S(1)}, bf16[1024,1024]{1,0:T(8,128)(2,1)}, u32[]{:S(2)}) copy-start(bf16[1024,1024]{1,0:T(8,128)(2,1)} %param.26) | copy-start | bytes 6291460
  7.2 8.3 copy-start.20
  7.2 8.3 copy-start.25
  7.2 179.9 %all-gather.23.cloned.1.call-start = ((), (), s32[]{:S(2)}) async-start(), calls=%async_computation.14 | async-start | bytes 23756800 | tf_op jit(solution)/shard_map/all_gather | solution.py:92
  9.8 9.3 copy-start.17
  26.8 2.1 copy-start.27
  38.9 12.4 %copy-start.8 = (f32[2,577,4,64]{1,3,2,0:T(8,128)}, f32[2,577,4,64]{1,3,2,0:T(8,128)S(1)}, u32[]{:S(2)}) copy-start(f32[2,577,4,64]{1,3,2,0:T(8,128)S(1)} %copy.107) | copy-start | bytes 3545092
  49.2 4.4 copy-start.1
  59.5 4.5 copy-start.31
  63.5 265.2 %all-reduce.15.cloned.1.call-start = ((), (), s32[]{:S(2)}) async-start(), calls=%async_computation.5 | async-start | bytes 9502720 | tf_op jit(solution)/shard_map/psum | solution.py:108
  198.6 5.0 copy-start.19
  203.6 4.2 copy-start.2
  203.6 5.2 copy-start.5
  210.1 7.7 copy-start.24
  210.1 7.7 copy-start.29
  210.1 7.7 copy-start.30
  210.1 13.7 %slice-start.2 = ((s8[4751360]{0:T(1024)(128)(4,1)}), s8[557056]{0:T(1024)(128)(4,1)S(1)}, s32[]{:S(2)}) async-start(s8[4751360]{0:T(1024)(128)(4,1)} %bitcast.72), calls=%async_computation.20 | async-start | bytes 1114112
  217.9 5.9 slice-start.3
  223.8 4.4 copy-start.33
  223.8 5.8 copy-start.28
  228.2 1.4 copy-start.34
  234.0 189.8 %reduce-scatter.10.cloned.1.call-start = ((), (), s32[]{:S(2)}) async-start(), calls=%async_computation.8 | async-start | bytes 1572864 | tf_op jit(solution)/shard_map/reduce_scatter | solution.py:151
  328.7 5.5 copy-start.7
  328.7 9.4 slice-start.4
  334.2 3.9 slice-start.5
  338.7 2.1 copy-start.3
  342.7 81.1 %reduce-scatter.12.cloned.1.call-start = ((), (), s32[]{:S(2)}) async-start(), calls=%async_computation.10 | async-start | bytes 6291456 | tf_op jit(solution)/shard_map/reduce_scatter | solution.py:155
  351.3 9.0 copy-start.14
  351.3 126.4 %reduce-scatter.14.cloned.1.call-start = ((), (), s32[]{:S(2)}) async-start(), calls=%async_computation.12 | async-start | bytes 6291456 | tf_op jit(solution)/shard_map/reduce_scatter | solution.py:157
  360.2 163.6 %reduce-scatter.8.cloned.1.call-start = ((), (), s32[]{:S(2)}) async-start(), calls=%async_computation.6 | async-start | bytes 4718592 | tf_op jit(solution)/shard_map/reduce_scatter | solution.py:149
  368.4 13.8 %copy-start.9 = (f32[2,577,4,64]{1,3,2,0:T(8,128)S(1)}, f32[2,577,4,64]{1,3,2,0:T(8,128)}, u32[]{:S(2)}) copy-start(f32[2,577,4,64]{1,3,2,0:T(8,128)} %copy-done.8) | copy-start | bytes 3545092
  389.9 9.0 copy-start.10
  396.3 2.6 copy-start.4
  398.9 6.5 copy-start.11
  416.8 1.2 copy-start.16
  423.7 325.6 %all-reduce.19.cloned.1.call-start = ((), (), s32[]{:S(2)}) async-start(), calls=%async_computation.17 | async-start | bytes 12582912 | tf_op jit(solution)/shard_map/psum | solution.py:160
  523.9 237.6 %reduce-scatter.16.cloned.1.call-start = ((), (), s32[]{:S(2)}) async-start(), calls=%async_computation.15 | async-start | bytes 196608
  531.7 403.3 %all-reduce.17.cloned.1.call-start = ((), (), s32[]{:S(2)}) async-start(), calls=%async_computation.16 | async-start | bytes 19005440 | tf_op jit(solution)/shard_map/psum | solution.py:97
  538.5 212.9 %copy-start.18 = (f32[2,577]{1,0:T(2,128)S(1)}, f32[2,577]{1,0:T(2,128)}, u32[]{:S(2)}) copy-start(f32[2,577]{1,0:T(2,128)} %copy-done.17) | copy-start | bytes 13852
  538.5 213.0 %copy-start.22 = (f32[2,577]{1,0:T(2,128)S(1)}, f32[2,577]{1,0:T(2,128)}, u32[]{:S(2)}) copy-start(f32[2,577]{1,0:T(2,128)} %get-tuple-element.109) | copy-start | bytes 13852
  538.5 213.1 %copy-start.32 = (u32[32]{0:T(128)S(1)}, u32[32]{0:T(128)}, u32[]{:S(2)}) copy-start(u32[32]{0:T(128)} %constant.32) | copy-start | bytes 388
  538.6 396.5 %copy-start.26 = (f32[1024]{0:T(1024)S(1)}, f32[1024]{0:T(1024)}, u32[]{:S(2)}) copy-start(f32[1024]{0:T(1024)} %param.27) | copy-start | bytes 12292
  538.6 495.8 %all-gather.17.cloned.1.call-start = ((), (), s32[]{:S(2)}) async-start(), calls=%async_computation.9 | async-start | bytes 1572864 | tf_op jit(solution)/shard_map/all_gather | solution.py:196
  749.4 285.0 %all-gather.15.cloned.1.call-start = ((), (), s32[]{:S(2)}) async-start(), calls=%async_computation.7 | async-start | bytes 4718592 | tf_op jit(solution)/shard_map/all_gather | solution.py:194
  750.1 312.7 %all-gather.19.cloned.1.call-start = ((), (), s32[]{:S(2)}) async-start(), calls=%async_computation.11 | async-start | bytes 6291456 | tf_op jit(solution)/shard_map/all_gather | solution.py:200
  750.7 370.4 %all-gather.21.cloned.1.call-start = ((), (), s32[]{:S(2)}) async-start(), calls=%async_computation.13 | async-start | bytes 6291456 | tf_op jit(solution)/shard_map/all_gather | solution.py:202
  941.5 9.4 copy-start.21
  945.2 5.7 copy-start.6
  950.9 4.3 copy-start.23
  950.9 72.5 %slice-start = ((s8[4751360]{0:T(1024)(128)(4,1)}), s8[557056]{0:T(1024)(128)(4,1)S(1)}, s32[]{:S(2)}) async-start(s8[4751360]{0:T(1024)(128)(4,1)} %bitcast.70), calls=%async_computation.18 | async-start | bytes 1114112
  1018.3 5.1 slice-start.1
  1034.4 92.3 %copy-start.15 = (f32[256,1024]{1,0:T(8,128)S(1)}, f32[256,1024]{1,0:T(8,128)}, u32[]{:S(2)}) copy-start(f32[256,1024]{1,0:T(8,128)} %all-gather.17.cloned.1.call-done) | copy-start | bytes 3145732
  1121.1 8.4 copy-start.12
  1126.7 5.4 copy-start.13
Sparse Core Ops, SparseCore 0:
  63.7 123.4 all-gather.22
  234.1 94.5 all-reduce.14
  342.8 20.5 reduce-scatter.9
  366.2 54.3 reduce-scatter.11
  423.3 54.3 reduce-scatter.13
  480.4 43.4 reduce-scatter.7
  526.5 222.8 all-reduce.18
  752.1 9.2 reduce-scatter.15
  764.0 170.9 all-reduce.16
  936.4 21.4 all-gather.16
  959.4 45.1 all-gather.14
  1006.0 56.7 all-gather.18
  1064.3 56.6 all-gather.20
